TPU v7x, 512 devices: a whole 4x4x16 slice. The times are simulated.
512 devices in a mesh: dp: 64 (over z, x_hi, core), fsdp: 8 (over x_lo, y).
Axes of the slice: x: 4 (x_hi: 2, x_lo: 2; x = x_hi * 2 + x_lo), y: 4, z: 16, core: 2. Of those that a mesh axis runs over, the one named last changes fastest.
Arguments:
- states: bfloat16 [128, 512, 5120], P('dp', None, 'fsdp'), may hold values from -240 to 240
- valid_counts: int32 [128], P('dp'), may hold values from 32 to 512
- section_ids: int32 [128], replicated, may hold values from 0 to 63, never falling along the last dimension, each value on 1 to 6 neighbouring positions
- norm_gain: bfloat16 [5120], P('fsdp'), may hold values from 0.099609375 to 1.8984375
- head_weight: bfloat16 [5120, 2048], P('fsdp'), may hold values from -0.078125 to 0.078125
Outputs:
- embeddings: float32 [64, 3840], P('dp')
Inputs may be any that keep to these rules, and one draw needn't show every extreme that they name: `section_ids`: section numbers never fall along the spans; every one of the 64 sections has 1 to 6 spans.
All inputs are finite; a program needn't handle non-finite values.
Results may differ from a plain program's by a relative error of at most 0.0003.
Values sent between devices are 32-bit elements; how exact they have to be, the bound alone decides.
No kernel may reach another device: no remote copies, remote signals or barrier semaphores. Data moves between devices by JAX's collectives and lax.ppermute only.
A program may use at most 64 MiB of HBM per device.

v0:
```python
import jax
import jax.numpy as jnp
from jax import lax
from jax.sharding import PartitionSpec as P

D = 5120
epsilon = 1e-06


def nested(projected):
    width = projected.shape[1]
    pieces = []
    for level in (width // 8, width // 4, width // 2, width):
        front = projected[:, :level]
        pieces.append(front * lax.rsqrt(jnp.mean(front * front, axis=1, keepdims=True) + epsilon))
    return jnp.concatenate(pieces, axis=1)


def local(states, valid_counts, section_ids, norm_gain, head_weight):
    values = states.astype(jnp.float32)
    partial_squares = jnp.sum(values * values, axis=-1)
    squares = lax.psum(partial_squares, "fsdp")
    scale = lax.rsqrt(squares / D + epsilon)
    slots = jnp.arange(states.shape[1], dtype=jnp.int32)
    used = (slots[None, :] < valid_counts[:, None]).astype(jnp.float32)
    weights = scale * used
    sums = jnp.einsum("cl,cld->cd", weights, values, precision=lax.Precision.HIGHEST)
    pooled = (
        sums / valid_counts.astype(jnp.float32)[:, None] * norm_gain.astype(jnp.float32)[None, :]
    )
    groups = lax.axis_size("dp")
    local_spans = pooled.shape[0]
    sec_local = local_spans // 2
    total_sections = sec_local * groups
    labels = jnp.arange(total_sections, dtype=jnp.int32)
    columns = lax.all_to_all(pooled, "dp", split_axis=1, concat_axis=0, tiled=True)
    member = (section_ids[None, :] == labels[:, None]).astype(jnp.float32)
    section_sums = jnp.dot(member, columns, precision=lax.Precision.HIGHEST)
    width = columns.shape[1]
    weight_part = lax.dynamic_slice_in_dim(head_weight, lax.axis_index("dp") * width, width, 0)
    weight_rows = weight_part.astype(jnp.float32)
    terms = jnp.dot(section_sums, weight_rows, precision=lax.Precision.HIGHEST)
    summed = lax.psum(terms, ("dp", "fsdp"))
    start = lax.axis_index("dp") * sec_local
    projected = lax.dynamic_slice_in_dim(summed, start, sec_local, 0)
    return nested(projected)


def solution(mesh):
    in_specs = (P("dp", None, "fsdp"), P("dp"), P(), P("fsdp"), P("fsdp", None))
    out_specs = P("dp", None)
    return jax.shard_map(local, mesh=mesh, in_specs=in_specs, out_specs=out_specs, check_vma=False)
```

profile of v0, /device:TPU:4, one launch (start us, length us, event | category | flops | bytes accessed | tf_op | source)
XLA Modules:
  0.0 534.0 jit_solution(12853491107874853173)
XLA Ops:
  6.5 0.0 copy-start
  6.5 0.0 copy-start.1
  6.5 0.8 convert_element_type.13
  7.4 0.7 convert_element_type.14
  8.0 1.6 multiply_reduce_fusion
  9.7 19.6 %psum.14 = f32[2,512]{1,0:T(2,128)S(1)} all-reduce(f32[2,512]{1,0:T(2,128)S(1)} %multiply_reduce_fusion), channel_id=1, replica_groups=mesh['dp'=64,'fsdp'=8] {'fsdp'}, use_global_device_ids=true, to_apply=%region_1.0 | all-reduce | flops 1024 | bytes 8192 | tf_op jit(solution)/shard_map/psum | solution.py:22
  29.3 0.7 fusion.5
  30.0 1.9 fusion.6
  31.9 0.1 fusion.4
  32.0 0.1 all_to_all.14
  32.2 0.7 copy.7
  32.8 18.6 %all-to-all-start = ((f32[2,64,10]{2,0,1:T(2,128)}), f32[2,64,10]{2,0,1:T(2,128)S(1)}, u32[]{:S(2)}, u32[]{:S(2)}) async-start(f32[2,64,10]{2,0,1:T(2,128)} %copy.7), calls=%async_computation | async-start | bytes 131072 | tf_op jit(solution)/shard_map/all_to_all | solution.py:36
  51.5 0.0 all-reduce.2.cloned.1.call-start
  51.5 13.8 %all-to-all-done = f32[2,64,10]{2,0,1:T(2,128)S(1)} async-done(((f32[2,64,10]{2,0,1:T(2,128)}), f32[2,64,10]{2,0,1:T(2,128)S(1)}, u32[]{:S(2)}, u32[]{:S(2)}) %all-to-all-start) | async-done | bytes 5152 | tf_op jit(solution)/shard_map/all_to_all | solution.py:36
  65.3 0.0 copy-done.1
  65.3 0.2 fusion.2
  65.5 0.0 copy-done
  65.5 1.3 fusion
  66.8 0.0 all-reduce.2.cloned.1.call-update
  66.8 448.4 %all-reduce.2.cloned.1.call-done = f32[64,2048]{1,0:T(8,128)} async-done(((f32[64,2048]{1,0:T(8,128)}), f32[64,2048]{1,0:T(8,128)}) %all-reduce.2.cloned.1.call-update) | async-done | bytes 524304 | tf_op jit(solution)/shard_map/psum | solution.py:43
  515.2 1.5 multiply_reduce_fusion.1
  517.3 1.4 multiply_reduce_fusion.2
  519.4 1.3 multiply_reduce_fusion.3
  521.4 1.3 multiply_reduce_fusion.4
  523.4 0.7 broadcast_multiply_fusion.3
  524.1 0.7 broadcast_multiply_fusion.2
  524.9 0.8 broadcast_multiply_fusion.1
  525.6 0.9 broadcast_multiply_fusion
  526.5 0.6 pad_maximum_fusion
Async XLA Ops:
  6.5 59.0 %copy-start = (bf16[640,2048]{1,0:T(8,128)(2,1)S(1)}, bf16[640,2048]{1,0:T(8,128)(2,1)}, u32[]{:S(2)}) copy-start(bf16[640,2048]{1,0:T(8,128)(2,1)} %param.9) | copy-start | bytes 7864324
  6.5 58.8 %copy-start.1 = (s32[128]{0:T(128)S(1)}, s32[128]{0:T(128)}, u32[]{:S(2)}) copy-start(s32[128]{0:T(128)} %param.7) | copy-start | bytes 1540
  32.8 32.5 %all-to-all-start = ((f32[2,64,10]{2,0,1:T(2,128)}), f32[2,64,10]{2,0,1:T(2,128)S(1)}, u32[]{:S(2)}, u32[]{:S(2)}) async-start(f32[2,64,10]{2,0,1:T(2,128)} %copy.7), calls=%async_computation | async-start | bytes 131072 | tf_op jit(solution)/shard_map/all_to_all | solution.py:36
  51.5 463.7 %all-reduce.2.cloned.1.call-start = ((), (), s32[]{:S(2)}) async-start(), calls=%async_computation.1 | async-start | bytes 1048576 | tf_op jit(solution)/shard_map/psum | solution.py:43
Sparse Core Ops, SparseCore 0:
  66.9 448.2 all-reduce.1
where the time goes:
time: 535 us; the launch traced here: 534 us
  waiting for transfers between devices  462 us (86%)
  blocking collectives  19.6 us (4%)
  starting transfers between devices  18.7 us (3%)
  between operations  16.2 us (3%)
  other arithmetic  13.1 us (2%)
    psum x1, waiting for transfers between devices, local(): summed = lax.psum(terms, ('dp', 'fsdp'))  448 us
    psum x1, blocking collectives, local(): squares = lax.psum(partial_squares, 'fsdp')  19.6 us
    all_to_all x1, starting transfers between devices, local(): lax.all_to_all(pooled, 'dp', split_axis=1, concat_axis=0, tiled=True)  18.6 us
    all_to_all x1, waiting for transfers between devices, local(): lax.all_to_all(pooled, 'dp', split_axis=1, concat_axis=0, tiled=True)  13.8 us
  transfers between devices with their start and end apart: 2, of which 2 were waited for; matrix products, arithmetic and copies ran while one was open for 0% of the time, Pallas kernels for 0%

commit v1 on v0

--- a/solution.py
+++ b/solution.py
@@ -40,7 +40,8 @@
     weight_part = lax.dynamic_slice_in_dim(head_weight, lax.axis_index("dp") * width, width, 0)
     weight_rows = weight_part.astype(jnp.float32)
     terms = jnp.dot(section_sums, weight_rows, precision=lax.Precision.HIGHEST)
-    summed = lax.psum(terms, ("dp", "fsdp"))
+    inner = lax.psum(terms, "dp")
+    summed = lax.psum(inner, "fsdp")
     start = lax.axis_index("dp") * sec_local
     projected = lax.dynamic_slice_in_dim(summed, start, sec_local, 0)
     return nested(projected)

time: 535 us -> 691 us (1.29)
  waiting for transfers between devices: 462 us -> 619 us
    psum x1 -> x2, waiting for transfers between devices: 448 us -> 605 us  [the longest x1 512 us: local(): inner = lax.psum(terms, 'dp')]
  transfers between devices with their start and end apart: 2 -> 3, of which waited for: 2 -> 3; matrix products, arithmetic and copies ran while one was open for 0% -> 0% of each run, Pallas kernels for 0% -> 0%
where the time goes in v1:
time: 691 us; the launch traced here: 690 us
  waiting for transfers between devices  619 us (90%)
  blocking collectives  19.6 us (3%)
  starting transfers between devices  18.7 us (3%)
  between operations  16.2 us (2%)
  other arithmetic  13.1 us (2%)
    psum x1, waiting for transfers between devices, local(): inner = lax.psum(terms, 'dp')  512 us
    psum x1, waiting for transfers between devices, local(): summed = lax.psum(inner, 'fsdp')  92.5 us
    psum x1, blocking collectives, local(): squares = lax.psum(partial_squares, 'fsdp')  19.6 us
    all_to_all x1, starting transfers between devices, local(): lax.all_to_all(pooled, 'dp', split_axis=1, concat_axis=0, tiled=True)  18.6 us
  transfers between devices with their start and end apart: 3, of which 3 were waited for; matrix products, arithmetic and copies ran while one was open for 0% of the time, Pallas kernels for 0%

profile of v1, /device:TPU:4, one launch (start us, length us, event | category | flops | bytes accessed | tf_op | source)
XLA Modules:
  0.0 690.5 jit_solution(8173464733046810673)
XLA Ops:
  6.5 0.0 copy-start
  6.5 0.0 copy-start.1
  6.5 0.8 convert_element_type.13
  7.4 0.7 convert_element_type.14
  8.0 1.6 multiply_reduce_fusion
  9.7 19.6 %psum.21 = f32[2,512]{1,0:T(2,128)S(1)} all-reduce(f32[2,512]{1,0:T(2,128)S(1)} %multiply_reduce_fusion), channel_id=1, replica_groups=mesh['dp'=64,'fsdp'=8] {'fsdp'}, use_global_device_ids=true, to_apply=%region_1.0 | all-reduce | flops 1024 | bytes 8192 | tf_op jit(solution)/shard_map/psum | solution.py:22
  29.3 0.7 fusion.5
  30.0 1.9 fusion.6
  31.9 0.1 fusion.4
  32.0 0.1 all_to_all.14
  32.2 0.7 copy.7
  32.8 18.6 %all-to-all-start = ((f32[2,64,10]{2,0,1:T(2,128)}), f32[2,64,10]{2,0,1:T(2,128)S(1)}, u32[]{:S(2)}, u32[]{:S(2)}) async-start(f32[2,64,10]{2,0,1:T(2,128)} %copy.7), calls=%async_computation | async-start | bytes 131072 | tf_op jit(solution)/shard_map/all_to_all | solution.py:36
  51.5 0.0 all-reduce.3.cloned.1.call-start
  51.5 13.8 %all-to-all-done = f32[2,64,10]{2,0,1:T(2,128)S(1)} async-done(((f32[2,64,10]{2,0,1:T(2,128)}), f32[2,64,10]{2,0,1:T(2,128)S(1)}, u32[]{:S(2)}, u32[]{:S(2)}) %all-to-all-start) | async-done | bytes 5152 | tf_op jit(solution)/shard_map/all_to_all | solution.py:36
  65.3 0.0 copy-done.1
  65.3 0.2 fusion.2
  65.5 0.0 copy-done
  65.5 1.3 fusion
  66.8 0.0 all-reduce.3.cloned.1.call-update
  66.8 0.0 all-reduce.5.cloned.1.call-start
  66.8 512.3 %all-reduce.3.cloned.1.call-done = f32[64,2048]{1,0:T(8,128)} async-done(((f32[64,2048]{1,0:T(8,128)}), f32[64,2048]{1,0:T(8,128)}) %all-reduce.3.cloned.1.call-update) | async-done | bytes 524304 | tf_op jit(solution)/shard_map/psum | solution.py:43
  579.1 0.0 all-reduce.5.cloned.1.call-update
  579.2 92.5 %all-reduce.5.cloned.1.call-done = f32[64,2048]{1,0:T(8,128)} async-done(((f32[64,2048]{1,0:T(8,128)}), f32[64,2048]{1,0:T(8,128)}) %all-reduce.5.cloned.1.call-update) | async-done | bytes 524304 | tf_op jit(solution)/shard_map/psum | solution.py:44
  671.7 1.5 multiply_reduce_fusion.1
  673.9 1.4 multiply_reduce_fusion.2
  675.9 1.3 multiply_reduce_fusion.3
  678.0 1.3 multiply_reduce_fusion.4
  680.0 0.7 broadcast_multiply_fusion.3
  680.7 0.7 broadcast_multiply_fusion.2
  681.4 0.8 broadcast_multiply_fusion.1
  682.2 0.9 broadcast_multiply_fusion
  683.0 0.6 pad_maximum_fusion
Async XLA Ops:
  6.5 59.0 %copy-start = (bf16[640,2048]{1,0:T(8,128)(2,1)S(1)}, bf16[640,2048]{1,0:T(8,128)(2,1)}, u32[]{:S(2)}) copy-start(bf16[640,2048]{1,0:T(8,128)(2,1)} %param.9) | copy-start | bytes 7864324
  6.5 58.8 %copy-start.1 = (s32[128]{0:T(128)S(1)}, s32[128]{0:T(128)}, u32[]{:S(2)}) copy-start(s32[128]{0:T(128)} %param.7) | copy-start | bytes 1540
  32.8 32.5 %all-to-all-start = ((f32[2,64,10]{2,0,1:T(2,128)}), f32[2,64,10]{2,0,1:T(2,128)S(1)}, u32[]{:S(2)}, u32[]{:S(2)}) async-start(f32[2,64,10]{2,0,1:T(2,128)} %copy.7), calls=%async_computation | async-start | bytes 131072 | tf_op jit(solution)/shard_map/all_to_all | solution.py:36
  51.5 527.7 %all-reduce.3.cloned.1.call-start = ((), (), s32[]{:S(2)}) async-start(), calls=%async_computation.1 | async-start | bytes 1048576 | tf_op jit(solution)/shard_map/psum | solution.py:43
  66.8 604.9 %all-reduce.5.cloned.1.call-start = ((), (), s32[]{:S(2)}) async-start(), calls=%async_computation.2 | async-start | bytes 1048576 | tf_op jit(solution)/shard_map/psum | solution.py:44
Sparse Core Ops, SparseCore 0:
  66.9 512.1 all-reduce.2
  582.3 89.3 all-reduce.4
